TPU v7x, 32 devices: a whole 2x2x4 slice. The times are simulated.
32 devices in a mesh: parts: 2 (over y), cols: 4 (over z), rows: 2 (over x), rep: 2 (over core).
Axes of the slice: x: 2, y: 2, z: 4, core: 2. Of those that a mesh axis runs over, the one named last changes fastest.
Arguments:
- sources: float32 [4096, 64], P(('parts', 'rows')), parts along dimension 0, may hold values from -11 to 11
- source_mass: float32 [4096], P(('parts', 'rows')), parts along dimension 0, may hold values from 0.2 to 5
- targets: float32 [4096, 64], P(('parts', 'cols', 'rep')), parts along dimension 0, may hold values from -6 to 6
- target_mass: float32 [4096], P(('parts', 'cols', 'rep')), parts along dimension 0, may hold values from 0.2 to 5
- fate_panel: float32 [4096, 64], P(('parts', 'cols', 'rep')), parts along dimension 0, may hold values from 0 to 1
Outputs:
- f_pot: float32 [4096], P(('parts', 'rows')), parts along dimension 0
- g_pot: float32 [4096], P(('parts', 'cols', 'rep')), parts along dimension 0
- fate_rows: float32 [4096, 64], P(('parts', 'rows', 'cols', 'rep')), parts along dimension 0
There are 2 independent parts, one for each index of `parts`. A program takes and returns all parts, laid end to end along the dimension named above; each array names one. Nothing has to cross between parts.
All inputs are finite; a program needn't handle non-finite values.
Results may differ from a plain program's by a relative error of at most 0.0003.
Values sent between devices are 32-bit elements; how exact they have to be, the bound alone decides.
No kernel may reach another device: no remote copies, remote signals or barrier semaphores. Data moves between devices by JAX's collectives and lax.ppermute only.
A program may use at most 64 MiB of HBM per device.

v0:
```python
import math
import jax
import jax.numpy as jnp
from jax import lax
from jax.sharding import PartitionSpec as P

ITERS = 8
entropic = 0.1
relaxed = 1.0 / 1.1


def pair_cost(lhs_rows, lhs_sq, rhs_rows, rhs_sq):
    products = lax.dot_general(
        lhs_rows,
        rhs_rows,
        (((1,), (1,)), ((), ())),
        precision=lax.Precision.HIGHEST,
        preferred_element_type=jnp.float32,
    )
    return (lhs_sq[:, None] + rhs_sq[None, :] - 2.0 * products) / lhs_rows.shape[1]


def row_potential(maxima, totals):
    whole_peak = lax.pmax(maxima, ("cols", "rep"))
    whole_total = lax.psum(totals * jnp.exp(maxima - whole_peak), ("cols", "rep"))
    return -relaxed * entropic * (whole_peak + jnp.log(whole_total))


def col_potential(maxima, totals):
    whole_peak = lax.pmax(maxima, "rows")
    whole_total = lax.psum(totals * jnp.exp(maxima - whole_peak), "rows")
    return -relaxed * entropic * (whole_peak + jnp.log(whole_total))


def body(sources, source_mass, targets, target_mass, fate_panel):
    src_count = sources.shape[0]
    tgt_count = targets.shape[0]
    feature_dim = sources.shape[1]
    all_sources = src_count * lax.axis_size("rows")
    all_targets = tgt_count * lax.axis_size(("cols", "rep"))
    log_a = jnp.log(source_mass / all_sources)
    log_b = jnp.log(target_mass / all_targets)
    src_sq = jnp.sum(sources * sources, axis=1)
    tgt_sq = jnp.sum(targets * targets, axis=1)
    row_size = math.gcd(src_count, 512)
    block_count = src_count // row_size
    src_blocks = sources.reshape(block_count, row_size, feature_dim)
    sq_blocks = src_sq.reshape(block_count, row_size)
    loga_blocks = log_a.reshape(block_count, row_size)

    def row_scores(packed, g_pot):
        return (
            log_b[None, :]
            + (g_pot[None, :] - pair_cost(packed[0], packed[1], targets, tgt_sq)) / entropic
        )

    g_pot = jnp.zeros((tgt_count,), jnp.float32)
    f_pot = jnp.zeros((src_count,), jnp.float32)
    for iteration in range(ITERS):

        def row_per_block(packed):
            scores = row_scores(packed, g_pot)
            maxima = jnp.max(scores, axis=1)
            return (maxima, jnp.sum(jnp.exp(scores - maxima[:, None]), axis=1))

        maxima, row_totals = lax.map(row_per_block, (src_blocks, sq_blocks))
        maxima, totals = (maxima.reshape(src_count), row_totals.reshape(src_count))
        f_pot = row_potential(maxima, totals)
        f_blocks = f_pot.reshape(block_count, row_size)

        def col_per_block(running, packed):
            scores = (
                packed[2][:, None]
                + (packed[3][:, None] - pair_cost(packed[0], packed[1], targets, tgt_sq)) / entropic
            )
            highest = jnp.maximum(running[0], jnp.max(scores, axis=0))
            totals = running[1] * jnp.exp(running[0] - highest) + jnp.sum(
                jnp.exp(scores - highest[None, :]), axis=0
            )
            return ((highest, totals), None)

        initial = (
            jnp.full((tgt_count,), -jnp.inf, jnp.float32),
            jnp.zeros((tgt_count,), jnp.float32),
        )
        running, unused = lax.scan(
            col_per_block, initial, (src_blocks, sq_blocks, loga_blocks, f_blocks)
        )
        maxima, totals = running
        g_pot = col_potential(maxima, totals)

    def fate_block(packed):
        scores = row_scores(packed, g_pot)
        maxima = jnp.max(scores, axis=1)
        weights = jnp.exp(scores - maxima[:, None])
        totals = jnp.sum(weights, axis=1)
        weighted = jnp.dot(
            weights, fate_panel, precision=lax.Precision.HIGHEST, preferred_element_type=jnp.float32
        )
        return (maxima, totals, weighted)

    maxima, totals, weighted = lax.map(fate_block, (src_blocks, sq_blocks))
    maxima = maxima.reshape(src_count)
    totals = totals.reshape(src_count)
    weighted = weighted.reshape(src_count, fate_panel.shape[1])
    whole_peak = lax.pmax(maxima, ("cols", "rep"))
    factor = jnp.exp(maxima - whole_peak)
    part_weighted, part_total = (
        lax.psum_scatter(
            weighted * factor[:, None], ("cols", "rep"), scatter_dimension=0, tiled=True
        ),
        lax.psum_scatter(totals * factor, ("cols", "rep"), scatter_dimension=0, tiled=True),
    )
    fate_rows = part_weighted / part_total[:, None]
    return (f_pot, g_pot, fate_rows)


def solution(mesh):
    in_specs = (
        P(("parts", "rows"), None),
        P(("parts", "rows")),
        P(("parts", "cols", "rep"), None),
        P(("parts", "cols", "rep")),
        P(("parts", "cols", "rep"), None),
    )
    out_specs = (
        P(("parts", "rows")),
        P(("parts", "cols", "rep")),
        P(("parts", "rows", "cols", "rep"), None),
    )
    return jax.shard_map(body, mesh=mesh, in_specs=in_specs, out_specs=out_specs, check_vma=False)
```

profile of v0, /device:TPU:0, one launch (start us, length us, event | category | flops | bytes accessed | tf_op | source)
XLA Modules:
  0.0 399.3 jit_solution(12835680924114328844)
XLA Ops:
  11.3 18.1 %pmax.119 = f32[1024]{0:T(1024)S(1)} all-reduce(f32[1024]{0:T(1024)S(1)} %bitcast.428), channel_id=1, replica_groups=mesh['parts'=2,'cols'=4,'rows'=2,'rep'=2] {'cols','rep'}, use_global_device_ids=true, to_apply=%region_6.7 | all-reduce | flops 1024 | bytes 8192 | tf_op jit(solution)/shard_map/pmax | solution.py:24
  29.5 13.6 %psum.112 = f32[1024]{0:T(1024)S(1)} all-reduce(f32[1024]{0:T(1024)S(1)} %exponential_multiply_fusion.7), channel_id=1, replica_groups=mesh['parts'=2,'cols'=4,'rows'=2,'rep'=2] {'cols','rep'}, use_global_device_ids=true, to_apply=%region_7.8 | all-reduce | flops 1024 | bytes 8192 | tf_op jit(solution)/shard_map/psum | solution.py:25
  44.8 4.9 %pmax.120 = f32[256]{0:T(256)S(1)} all-reduce(f32[256]{0:T(256)S(1)} %get-tuple-element.827), channel_id=1, replica_groups=mesh['parts'=2,'cols'=4,'rows'=2,'rep'=2] {'rows'}, use_global_device_ids=true, to_apply=%region_12.13 | all-reduce | flops 256 | bytes 2048 | tf_op jit(solution)/shard_map/pmax | solution.py:30
  49.7 4.9 %psum.113 = f32[256]{0:T(256)S(1)} all-reduce(f32[256]{0:T(256)S(1)} %exponential_multiply_fusion.15), channel_id=1, replica_groups=mesh['parts'=2,'cols'=4,'rows'=2,'rep'=2] {'rows'}, use_global_device_ids=true, to_apply=%region_13.14 | all-reduce | flops 256 | bytes 2048 | tf_op jit(solution)/shard_map/psum | solution.py:31
  56.6 13.6 %pmax.121 = f32[1024]{0:T(1024)S(1)} all-reduce(f32[1024]{0:T(1024)S(1)} %bitcast.430), channel_id=1, replica_groups=mesh['parts'=2,'cols'=4,'rows'=2,'rep'=2] {'cols','rep'}, use_global_device_ids=true, to_apply=%region_18.19 | all-reduce | flops 1024 | bytes 8192 | tf_op jit(solution)/shard_map/pmax | solution.py:24
  70.2 13.6 %psum.114 = f32[1024]{0:T(1024)S(1)} all-reduce(f32[1024]{0:T(1024)S(1)} %exponential_multiply_fusion.6), channel_id=1, replica_groups=mesh['parts'=2,'cols'=4,'rows'=2,'rep'=2] {'cols','rep'}, use_global_device_ids=true, to_apply=%region_19.20 | all-reduce | flops 1024 | bytes 8192 | tf_op jit(solution)/shard_map/psum | solution.py:25
  85.6 4.9 %pmax.122 = f32[256]{0:T(256)S(1)} all-reduce(f32[256]{0:T(256)S(1)} %get-tuple-element.831), channel_id=1, replica_groups=mesh['parts'=2,'cols'=4,'rows'=2,'rep'=2] {'rows'}, use_global_device_ids=true, to_apply=%region_24.25 | all-reduce | flops 256 | bytes 2048 | tf_op jit(solution)/shard_map/pmax | solution.py:30
  97.4 13.6 %pmax.123 = f32[1024]{0:T(1024)S(1)} all-reduce(f32[1024]{0:T(1024)S(1)} %bitcast.432), channel_id=1, replica_groups=mesh['parts'=2,'cols'=4,'rows'=2,'rep'=2] {'cols','rep'}, use_global_device_ids=true, to_apply=%region_30.31 | all-reduce | flops 1024 | bytes 8192 | tf_op jit(solution)/shard_map/pmax | solution.py:24
  111.0 13.6 %psum.116 = f32[1024]{0:T(1024)S(1)} all-reduce(f32[1024]{0:T(1024)S(1)} %exponential_multiply_fusion.5), channel_id=1, replica_groups=mesh['parts'=2,'cols'=4,'rows'=2,'rep'=2] {'cols','rep'}, use_global_device_ids=true, to_apply=%region_31.32 | all-reduce | flops 1024 | bytes 8192 | tf_op jit(solution)/shard_map/psum | solution.py:25
  126.4 4.9 %pmax.124 = f32[256]{0:T(256)S(1)} all-reduce(f32[256]{0:T(256)S(1)} %get-tuple-element.835), channel_id=1, replica_groups=mesh['parts'=2,'cols'=4,'rows'=2,'rep'=2] {'rows'}, use_global_device_ids=true, to_apply=%region_36.37 | all-reduce | flops 256 | bytes 2048 | tf_op jit(solution)/shard_map/pmax | solution.py:30
  138.2 13.6 %pmax.125 = f32[1024]{0:T(1024)S(1)} all-reduce(f32[1024]{0:T(1024)S(1)} %bitcast.434), channel_id=1, replica_groups=mesh['parts'=2,'cols'=4,'rows'=2,'rep'=2] {'cols','rep'}, use_global_device_ids=true, to_apply=%region_42.43 | all-reduce | flops 1024 | bytes 8192 | tf_op jit(solution)/shard_map/pmax | solution.py:24
  151.8 13.6 %psum.118 = f32[1024]{0:T(1024)S(1)} all-reduce(f32[1024]{0:T(1024)S(1)} %exponential_multiply_fusion.4), channel_id=1, replica_groups=mesh['parts'=2,'cols'=4,'rows'=2,'rep'=2] {'cols','rep'}, use_global_device_ids=true, to_apply=%region_43.44 | all-reduce | flops 1024 | bytes 8192 | tf_op jit(solution)/shard_map/psum | solution.py:25
  167.2 4.9 %pmax.126 = f32[256]{0:T(256)S(1)} all-reduce(f32[256]{0:T(256)S(1)} %get-tuple-element.839), channel_id=1, replica_groups=mesh['parts'=2,'cols'=4,'rows'=2,'rep'=2] {'rows'}, use_global_device_ids=true, to_apply=%region_48.49 | all-reduce | flops 256 | bytes 2048 | tf_op jit(solution)/shard_map/pmax | solution.py:30
  179.0 13.6 %pmax.127 = f32[1024]{0:T(1024)S(1)} all-reduce(f32[1024]{0:T(1024)S(1)} %bitcast.436), channel_id=1, replica_groups=mesh['parts'=2,'cols'=4,'rows'=2,'rep'=2] {'cols','rep'}, use_global_device_ids=true, to_apply=%region_54.55 | all-reduce | flops 1024 | bytes 8192 | tf_op jit(solution)/shard_map/pmax | solution.py:24
  192.6 13.6 %psum.120 = f32[1024]{0:T(1024)S(1)} all-reduce(f32[1024]{0:T(1024)S(1)} %exponential_multiply_fusion.3), channel_id=1, replica_groups=mesh['parts'=2,'cols'=4,'rows'=2,'rep'=2] {'cols','rep'}, use_global_device_ids=true, to_apply=%region_55.56 | all-reduce | flops 1024 | bytes 8192 | tf_op jit(solution)/shard_map/psum | solution.py:25
  208.0 4.9 %pmax.128 = f32[256]{0:T(256)S(1)} all-reduce(f32[256]{0:T(256)S(1)} %get-tuple-element.843), channel_id=1, replica_groups=mesh['parts'=2,'cols'=4,'rows'=2,'rep'=2] {'rows'}, use_global_device_ids=true, to_apply=%region_60.61 | all-reduce | flops 256 | bytes 2048 | tf_op jit(solution)/shard_map/pmax | solution.py:30
  212.9 5.1 %psum.121 = f32[256]{0:T(256)S(1)} all-reduce(f32[256]{0:T(256)S(1)} %exponential_multiply_fusion.11), channel_id=1, replica_groups=mesh['parts'=2,'cols'=4,'rows'=2,'rep'=2] {'rows'}, use_global_device_ids=true, to_apply=%region_61.62 | all-reduce | flops 256 | bytes 2048 | tf_op jit(solution)/shard_map/psum | solution.py:31
  220.0 13.6 %pmax.129 = f32[1024]{0:T(1024)S(1)} all-reduce(f32[1024]{0:T(1024)S(1)} %bitcast.438), channel_id=1, replica_groups=mesh['parts'=2,'cols'=4,'rows'=2,'rep'=2] {'cols','rep'}, use_global_device_ids=true, to_apply=%region_66.67 | all-reduce | flops 1024 | bytes 8192 | tf_op jit(solution)/shard_map/pmax | solution.py:24
  233.6 13.6 %psum.122 = f32[1024]{0:T(1024)S(1)} all-reduce(f32[1024]{0:T(1024)S(1)} %exponential_multiply_fusion.2), channel_id=1, replica_groups=mesh['parts'=2,'cols'=4,'rows'=2,'rep'=2] {'cols','rep'}, use_global_device_ids=true, to_apply=%region_67.68 | all-reduce | flops 1024 | bytes 8192 | tf_op jit(solution)/shard_map/psum | solution.py:25
  248.9 4.9 %pmax.130 = f32[256]{0:T(256)S(1)} all-reduce(f32[256]{0:T(256)S(1)} %get-tuple-element.847), channel_id=1, replica_groups=mesh['parts'=2,'cols'=4,'rows'=2,'rep'=2] {'rows'}, use_global_device_ids=true, to_apply=%region_72.73 | all-reduce | flops 256 | bytes 2048 | tf_op jit(solution)/shard_map/pmax | solution.py:30
  253.9 4.9 %psum.123 = f32[256]{0:T(256)S(1)} all-reduce(f32[256]{0:T(256)S(1)} %exponential_multiply_fusion.10), channel_id=1, replica_groups=mesh['parts'=2,'cols'=4,'rows'=2,'rep'=2] {'rows'}, use_global_device_ids=true, to_apply=%region_73.74 | all-reduce | flops 256 | bytes 2048 | tf_op jit(solution)/shard_map/psum | solution.py:31
  260.8 13.6 %pmax.131 = f32[1024]{0:T(1024)S(1)} all-reduce(f32[1024]{0:T(1024)S(1)} %bitcast.440), channel_id=1, replica_groups=mesh['parts'=2,'cols'=4,'rows'=2,'rep'=2] {'cols','rep'}, use_global_device_ids=true, to_apply=%region_78.79 | all-reduce | flops 1024 | bytes 8192 | tf_op jit(solution)/shard_map/pmax | solution.py:24
  274.4 13.6 %psum.124 = f32[1024]{0:T(1024)S(1)} all-reduce(f32[1024]{0:T(1024)S(1)} %exponential_multiply_fusion.1), channel_id=1, replica_groups=mesh['parts'=2,'cols'=4,'rows'=2,'rep'=2] {'cols','rep'}, use_global_device_ids=true, to_apply=%region_79.80 | all-reduce | flops 1024 | bytes 8192 | tf_op jit(solution)/shard_map/psum | solution.py:25
  289.7 4.9 %pmax.132 = f32[256]{0:T(256)S(1)} all-reduce(f32[256]{0:T(256)S(1)} %get-tuple-element.851), channel_id=1, replica_groups=mesh['parts'=2,'cols'=4,'rows'=2,'rep'=2] {'rows'}, use_global_device_ids=true, to_apply=%region_84.85 | all-reduce | flops 256 | bytes 2048 | tf_op jit(solution)/shard_map/pmax | solution.py:30
  301.6 13.6 %pmax.133 = f32[1024]{0:T(1024)S(1)} all-reduce(f32[1024]{0:T(1024)S(1)} %bitcast.442), channel_id=1, replica_groups=mesh['parts'=2,'cols'=4,'rows'=2,'rep'=2] {'cols','rep'}, use_global_device_ids=true, to_apply=%region_90.91 | all-reduce | flops 1024 | bytes 8192 | tf_op jit(solution)/shard_map/pmax | solution.py:24
  315.2 13.6 %psum.126 = f32[1024]{0:T(1024)S(1)} all-reduce(f32[1024]{0:T(1024)S(1)} %exponential_multiply_fusion), channel_id=1, replica_groups=mesh['parts'=2,'cols'=4,'rows'=2,'rep'=2] {'cols','rep'}, use_global_device_ids=true, to_apply=%region_91.92 | all-reduce | flops 1024 | bytes 8192 | tf_op jit(solution)/shard_map/psum | solution.py:25
  331.1 4.9 %pmax.134 = f32[256]{0:T(256)S(1)} all-reduce(f32[256]{0:T(256)S(1)} %get-tuple-element.855), channel_id=1, replica_groups=mesh['parts'=2,'cols'=4,'rows'=2,'rep'=2] {'rows'}, use_global_device_ids=true, to_apply=%region_96.97 | all-reduce | flops 256 | bytes 2048 | tf_op jit(solution)/shard_map/pmax | solution.py:30
  336.0 4.9 %psum.127 = f32[256]{0:T(256)S(1)} all-reduce(f32[256]{0:T(256)S(1)} %exponential_multiply_fusion.8), channel_id=1, replica_groups=mesh['parts'=2,'cols'=4,'rows'=2,'rep'=2] {'rows'}, use_global_device_ids=true, to_apply=%region_97.98 | all-reduce | flops 256 | bytes 2048 | tf_op jit(solution)/shard_map/psum | solution.py:31
  341.0 5.7 %while.222 = (s32[]{:T(128)}, f32[2,512]{1,0:T(2,128)S(1)}, f32[2,512]{1,0:T(2,128)S(1)}, f32[2,512,64]{1,0,2:T(2,128)S(1)}, f32[256]{0:T(256)S(1)}, /*index=5*/...) while((s32[]{:T(128)}, f32[2,512]{1,0:T(2,128)S(1)}, ...), condition=%wide.region_101.102_spmd, body=%wide.region_98.101_spmd.sunk | while | flops 202767360 | bytes 2647193 | solution.py:102
  347.3 13.6 %pmax.135 = f32[1024]{0:T(1024)S(1)} all-reduce(f32[1024]{0:T(1024)S(1)} %bitcast.426), channel_id=1, replica_groups=mesh['parts'=2,'cols'=4,'rows'=2,'rep'=2] {'cols','rep'}, use_global_device_ids=true, to_apply=%region_102.103 | all-reduce | flops 1024 | bytes 8192 | tf_op jit(solution)/shard_map/pmax | solution.py:106
  363.6 13.7 %all-reduce = f32[1024]{0:T(1024)S(1)} all-reduce(f32[1024]{0:T(1024)S(1)} %get-tuple-element.1408), channel_id=3, replica_groups=mesh['parts'=2,'cols'=4,'rows'=2,'rep'=2] {'cols','rep'}, use_global_device_ids=true, to_apply=%region_104.105.clone | all-reduce | flops 1024 | bytes 8192
  377.3 13.7 %reduce-scatter.2.cloned.1.call-done = f32[128,64]{0,1:T(8,128)} async-done(((f32[1024,64]{0,1:T(8,128)}), f32[128,64]{0,1:T(8,128)}) %reduce-scatter.2.cloned.1.call-update) | async-done | bytes 32784 | tf_op jit(solution)/shard_map/reduce_scatter | solution.py:109
  (352 shorter events, 89.6 us)
Async XLA Ops:
  7.2 1.2 copy-start.1
  7.2 383.9 %reduce-scatter.2.cloned.1.call-start = ((), (), s32[]{:S(2)}) async-start(), calls=%async_computation.1 | async-start | bytes 294912 | tf_op jit(solution)/shard_map/reduce_scatter | solution.py:109
  8.4 1.0 copy-start.2
  8.6 0.7 copy-start.4
  8.6 0.7 copy-start.6
  328.8 0.6 copy-start.3
  329.4 11.6 %copy-start = (f32[256,64]{0,1:T(8,128)S(1)}, f32[256,64]{0,1:T(8,128)}, u32[]{:S(2)}) copy-start(f32[256,64]{0,1:T(8,128)} %param.43) | copy-start | bytes 196612
  346.7 0.6 copy-start.5
  361.7 0.7 copy-start.7
Sparse Core Ops, SparseCore 0:
  361.8 29.2 reduce-scatter.1
where the time goes:
time: 400 us; the launch traced here: 399 us
  blocking collectives  328 us (82%)
  matrix products  24.7 us (6%)
  between operations  15.2 us (4%)
  waiting for transfers between devices  13.8 us (3%)
  local copies, waits for them, and re-layouts  8.2 us (2%)
  other arithmetic  7.79 us (2%)
    pmax x8, blocking collectives, row_potential(): whole_peak = lax.pmax(maxima, ('cols', 'rep'))  113 us
    psum x8, blocking collectives, row_potential(): lax.psum(totals * jnp.exp(maxima - whole_peak), ('cols', 'rep'))  109 us
    psum x8, blocking collectives, col_potential(): whole_total = lax.psum(totals * jnp.exp(maxima - whole_peak), 'rows')  39.5 us
    pmax x8, blocking collectives, col_potential(): whole_peak = lax.pmax(maxima, 'rows')  39.5 us
    dot_general x34, matrix products, pair_cost(): lax.dot_general(lhs_rows, rhs_rows, (((1,), (1,)), ((), ())), precision=l...  23.7 us
    reduce_scatter x1, waiting for transfers between devices, body(): lax.psum_scatter(weighted * factor[:, None], ('cols', 'rep'), scatter_dim...  13.7 us
    unnamed x1, blocking collectives  13.7 us
    pmax x1, blocking collectives, body(): whole_peak = lax.pmax(maxima, ('cols', 'rep'))  13.6 us
  transfers between devices with their start and end apart: 1, of which 1 were waited for; matrix products, arithmetic and copies ran while one was open for 0% of the time, Pallas kernels for 0%

commit v1 on v0

--- a/solution.py
+++ b/solution.py
@@ -28,7 +28,9 @@
 
 def col_potential(maxima, totals):
     whole_peak = lax.pmax(maxima, "rows")
-    whole_total = lax.psum(totals * jnp.exp(maxima - whole_peak), "rows")
+    part = totals * jnp.exp(maxima - whole_peak)
+    terms = lax.all_gather(part, "rows")
+    whole_total = jnp.sum(terms, axis=0)
     return -relaxed * entropic * (whole_peak + jnp.log(whole_total))
 
 

time: 400 us -> 395 us (0.988)
  blocking collectives: 328 us -> 323 us
    psum x8 -> x0, blocking collectives: 39.5 us -> none  [col_potential(): whole_total = lax.psum(totals * jnp.exp(maxima - whole_peak), 'rows')]
    all_gather x0 -> x8, blocking collectives: none -> 34.1 us  [col_potential(): terms = lax.all_gather(part, 'rows')]
where the time goes in v1:
time: 395 us; the launch traced here: 394 us
  blocking collectives  323 us (82%)
  matrix products  24.7 us (6%)
  between operations  15.3 us (4%)
  waiting for transfers between devices  13.6 us (3%)
  local copies, waits for them, and re-layouts  8.21 us (2%)
  other arithmetic  7.95 us (2%)
    pmax x8, blocking collectives, row_potential(): whole_peak = lax.pmax(maxima, ('cols', 'rep'))  113 us
    psum x8, blocking collectives, row_potential(): lax.psum(totals * jnp.exp(maxima - whole_peak), ('cols', 'rep'))  109 us
    pmax x8, blocking collectives, col_potential(): whole_peak = lax.pmax(maxima, 'rows')  39.5 us
    all_gather x8, blocking collectives, col_potential(): terms = lax.all_gather(part, 'rows')  34.1 us
    dot_general x34, matrix products, pair_cost(): lax.dot_general(lhs_rows, rhs_rows, (((1,), (1,)), ((), ())), precision=l...  23.7 us
    unnamed x1, blocking collectives  13.7 us
    pmax x1, blocking collectives, body(): whole_peak = lax.pmax(maxima, ('cols', 'rep'))  13.6 us
    reduce_scatter x1, waiting for transfers between devices, body(): lax.psum_scatter(weighted * factor[:, None], ('cols', 'rep'), scatter_dim...  13.6 us
  transfers between devices with their start and end apart: 1, of which 1 were waited for; matrix products, arithmetic and copies ran while one was open for 0% of the time, Pallas kernels for 0%

profile of v1, /device:TPU:0, one launch (start us, length us, event | category | flops | bytes accessed | tf_op | source)
XLA Modules:
  0.0 393.9 jit_solution(7241451888707832330)
XLA Ops:
  11.3 18.1 %pmax.119 = f32[1024]{0:T(1024)S(1)} all-reduce(f32[1024]{0:T(1024)S(1)} %bitcast.436), channel_id=1, replica_groups=mesh['parts'=2,'cols'=4,'rows'=2,'rep'=2] {'cols','rep'}, use_global_device_ids=true, to_apply=%region_6.7 | all-reduce | flops 1024 | bytes 8192 | tf_op jit(solution)/shard_map/pmax | solution.py:24
  29.5 13.6 %psum.56 = f32[1024]{0:T(1024)S(1)} all-reduce(f32[1024]{0:T(1024)S(1)} %exponential_multiply_fusion.7), channel_id=1, replica_groups=mesh['parts'=2,'cols'=4,'rows'=2,'rep'=2] {'cols','rep'}, use_global_device_ids=true, to_apply=%region_7.8 | all-reduce | flops 1024 | bytes 8192 | tf_op jit(solution)/shard_map/psum | solution.py:25
  44.8 4.9 %pmax.120 = f32[256]{0:T(256)S(1)} all-reduce(f32[256]{0:T(256)S(1)} %get-tuple-element.827), channel_id=1, replica_groups=mesh['parts'=2,'cols'=4,'rows'=2,'rep'=2] {'rows'}, use_global_device_ids=true, to_apply=%region_12.13 | all-reduce | flops 256 | bytes 2048 | tf_op jit(solution)/shard_map/pmax | solution.py:30
  49.7 4.2 %all-gather.8 = f32[2,1,256]{2,1,0:T(1,128)S(1)} all-gather(f32[1,1,256]{2,1,0:T(1,128)S(1)} %bitcast.479), channel_id=2, replica_groups=mesh['parts'=2,'cols'=4,'rows'=2,'rep'=2] {'rows'}, dimensions={0}, use_global_device_ids=true | all-gather | bytes 3072 | tf_op jit(solution)/shard_map/all_gather | solution.py:32
  56.0 13.6 %pmax.121 = f32[1024]{0:T(1024)S(1)} all-reduce(f32[1024]{0:T(1024)S(1)} %bitcast.438), channel_id=1, replica_groups=mesh['parts'=2,'cols'=4,'rows'=2,'rep'=2] {'cols','rep'}, use_global_device_ids=true, to_apply=%region_18.19 | all-reduce | flops 1024 | bytes 8192 | tf_op jit(solution)/shard_map/pmax | solution.py:24
  69.6 13.6 %psum.57 = f32[1024]{0:T(1024)S(1)} all-reduce(f32[1024]{0:T(1024)S(1)} %exponential_multiply_fusion.6), channel_id=1, replica_groups=mesh['parts'=2,'cols'=4,'rows'=2,'rep'=2] {'cols','rep'}, use_global_device_ids=true, to_apply=%region_19.20 | all-reduce | flops 1024 | bytes 8192 | tf_op jit(solution)/shard_map/psum | solution.py:25
  84.9 4.9 %pmax.122 = f32[256]{0:T(256)S(1)} all-reduce(f32[256]{0:T(256)S(1)} %get-tuple-element.831), channel_id=1, replica_groups=mesh['parts'=2,'cols'=4,'rows'=2,'rep'=2] {'rows'}, use_global_device_ids=true, to_apply=%region_24.25 | all-reduce | flops 256 | bytes 2048 | tf_op jit(solution)/shard_map/pmax | solution.py:30
  89.9 4.2 %all-gather.9 = f32[2,1,256]{2,1,0:T(1,128)S(1)} all-gather(f32[1,1,256]{2,1,0:T(1,128)S(1)} %bitcast.480), channel_id=3, replica_groups=mesh['parts'=2,'cols'=4,'rows'=2,'rep'=2] {'rows'}, dimensions={0}, use_global_device_ids=true | all-gather | bytes 3072 | tf_op jit(solution)/shard_map/all_gather | solution.py:32
  96.1 13.6 %pmax.123 = f32[1024]{0:T(1024)S(1)} all-reduce(f32[1024]{0:T(1024)S(1)} %bitcast.440), channel_id=1, replica_groups=mesh['parts'=2,'cols'=4,'rows'=2,'rep'=2] {'cols','rep'}, use_global_device_ids=true, to_apply=%region_30.31 | all-reduce | flops 1024 | bytes 8192 | tf_op jit(solution)/shard_map/pmax | solution.py:24
  109.7 13.6 %psum.58 = f32[1024]{0:T(1024)S(1)} all-reduce(f32[1024]{0:T(1024)S(1)} %exponential_multiply_fusion.5), channel_id=1, replica_groups=mesh['parts'=2,'cols'=4,'rows'=2,'rep'=2] {'cols','rep'}, use_global_device_ids=true, to_apply=%region_31.32 | all-reduce | flops 1024 | bytes 8192 | tf_op jit(solution)/shard_map/psum | solution.py:25
  125.1 4.9 %pmax.124 = f32[256]{0:T(256)S(1)} all-reduce(f32[256]{0:T(256)S(1)} %get-tuple-element.835), channel_id=1, replica_groups=mesh['parts'=2,'cols'=4,'rows'=2,'rep'=2] {'rows'}, use_global_device_ids=true, to_apply=%region_36.37 | all-reduce | flops 256 | bytes 2048 | tf_op jit(solution)/shard_map/pmax | solution.py:30
  130.0 4.2 %all-gather.10 = f32[2,1,256]{2,1,0:T(1,128)S(1)} all-gather(f32[1,1,256]{2,1,0:T(1,128)S(1)} %bitcast.481), channel_id=4, replica_groups=mesh['parts'=2,'cols'=4,'rows'=2,'rep'=2] {'rows'}, dimensions={0}, use_global_device_ids=true | all-gather | bytes 3072 | tf_op jit(solution)/shard_map/all_gather | solution.py:32
  136.2 13.6 %pmax.125 = f32[1024]{0:T(1024)S(1)} all-reduce(f32[1024]{0:T(1024)S(1)} %bitcast.442), channel_id=1, replica_groups=mesh['parts'=2,'cols'=4,'rows'=2,'rep'=2] {'cols','rep'}, use_global_device_ids=true, to_apply=%region_42.43 | all-reduce | flops 1024 | bytes 8192 | tf_op jit(solution)/shard_map/pmax | solution.py:24
  149.9 13.6 %psum.59 = f32[1024]{0:T(1024)S(1)} all-reduce(f32[1024]{0:T(1024)S(1)} %exponential_multiply_fusion.4), channel_id=1, replica_groups=mesh['parts'=2,'cols'=4,'rows'=2,'rep'=2] {'cols','rep'}, use_global_device_ids=true, to_apply=%region_43.44 | all-reduce | flops 1024 | bytes 8192 | tf_op jit(solution)/shard_map/psum | solution.py:25
  165.2 4.9 %pmax.126 = f32[256]{0:T(256)S(1)} all-reduce(f32[256]{0:T(256)S(1)} %get-tuple-element.839), channel_id=1, replica_groups=mesh['parts'=2,'cols'=4,'rows'=2,'rep'=2] {'rows'}, use_global_device_ids=true, to_apply=%region_48.49 | all-reduce | flops 256 | bytes 2048 | tf_op jit(solution)/shard_map/pmax | solution.py:30
  176.4 13.6 %pmax.127 = f32[1024]{0:T(1024)S(1)} all-reduce(f32[1024]{0:T(1024)S(1)} %bitcast.444), channel_id=1, replica_groups=mesh['parts'=2,'cols'=4,'rows'=2,'rep'=2] {'cols','rep'}, use_global_device_ids=true, to_apply=%region_54.55 | all-reduce | flops 1024 | bytes 8192 | tf_op jit(solution)/shard_map/pmax | solution.py:24
  190.0 13.6 %psum.60 = f32[1024]{0:T(1024)S(1)} all-reduce(f32[1024]{0:T(1024)S(1)} %exponential_multiply_fusion.3), channel_id=1, replica_groups=mesh['parts'=2,'cols'=4,'rows'=2,'rep'=2] {'cols','rep'}, use_global_device_ids=true, to_apply=%region_55.56 | all-reduce | flops 1024 | bytes 8192 | tf_op jit(solution)/shard_map/psum | solution.py:25
  205.4 4.9 %pmax.128 = f32[256]{0:T(256)S(1)} all-reduce(f32[256]{0:T(256)S(1)} %get-tuple-element.843), channel_id=1, replica_groups=mesh['parts'=2,'cols'=4,'rows'=2,'rep'=2] {'rows'}, use_global_device_ids=true, to_apply=%region_60.61 | all-reduce | flops 256 | bytes 2048 | tf_op jit(solution)/shard_map/pmax | solution.py:30
  210.3 4.4 %all-gather.12 = f32[2,1,256]{2,1,0:T(1,128)S(1)} all-gather(f32[1,1,256]{2,1,0:T(1,128)S(1)} %bitcast.483), channel_id=6, replica_groups=mesh['parts'=2,'cols'=4,'rows'=2,'rep'=2] {'rows'}, dimensions={0}, use_global_device_ids=true | all-gather | bytes 3072 | tf_op jit(solution)/shard_map/all_gather | solution.py:32
  216.7 13.6 %pmax.129 = f32[1024]{0:T(1024)S(1)} all-reduce(f32[1024]{0:T(1024)S(1)} %bitcast.446), channel_id=1, replica_groups=mesh['parts'=2,'cols'=4,'rows'=2,'rep'=2] {'cols','rep'}, use_global_device_ids=true, to_apply=%region_66.67 | all-reduce | flops 1024 | bytes 8192 | tf_op jit(solution)/shard_map/pmax | solution.py:24
  230.3 13.6 %psum.61 = f32[1024]{0:T(1024)S(1)} all-reduce(f32[1024]{0:T(1024)S(1)} %exponential_multiply_fusion.2), channel_id=1, replica_groups=mesh['parts'=2,'cols'=4,'rows'=2,'rep'=2] {'cols','rep'}, use_global_device_ids=true, to_apply=%region_67.68 | all-reduce | flops 1024 | bytes 8192 | tf_op jit(solution)/shard_map/psum | solution.py:25
  245.7 4.9 %pmax.130 = f32[256]{0:T(256)S(1)} all-reduce(f32[256]{0:T(256)S(1)} %get-tuple-element.847), channel_id=1, replica_groups=mesh['parts'=2,'cols'=4,'rows'=2,'rep'=2] {'rows'}, use_global_device_ids=true, to_apply=%region_72.73 | all-reduce | flops 256 | bytes 2048 | tf_op jit(solution)/shard_map/pmax | solution.py:30
  256.9 13.6 %pmax.131 = f32[1024]{0:T(1024)S(1)} all-reduce(f32[1024]{0:T(1024)S(1)} %bitcast.448), channel_id=1, replica_groups=mesh['parts'=2,'cols'=4,'rows'=2,'rep'=2] {'cols','rep'}, use_global_device_ids=true, to_apply=%region_78.79 | all-reduce | flops 1024 | bytes 8192 | tf_op jit(solution)/shard_map/pmax | solution.py:24
  270.5 13.6 %psum.62 = f32[1024]{0:T(1024)S(1)} all-reduce(f32[1024]{0:T(1024)S(1)} %exponential_multiply_fusion.1), channel_id=1, replica_groups=mesh['parts'=2,'cols'=4,'rows'=2,'rep'=2] {'cols','rep'}, use_global_device_ids=true, to_apply=%region_79.80 | all-reduce | flops 1024 | bytes 8192 | tf_op jit(solution)/shard_map/psum | solution.py:25
  285.8 4.9 %pmax.132 = f32[256]{0:T(256)S(1)} all-reduce(f32[256]{0:T(256)S(1)} %get-tuple-element.851), channel_id=1, replica_groups=mesh['parts'=2,'cols'=4,'rows'=2,'rep'=2] {'rows'}, use_global_device_ids=true, to_apply=%region_84.85 | all-reduce | flops 256 | bytes 2048 | tf_op jit(solution)/shard_map/pmax | solution.py:30
  297.0 13.6 %pmax.133 = f32[1024]{0:T(1024)S(1)} all-reduce(f32[1024]{0:T(1024)S(1)} %bitcast.450), channel_id=1, replica_groups=mesh['parts'=2,'cols'=4,'rows'=2,'rep'=2] {'cols','rep'}, use_global_device_ids=true, to_apply=%region_90.91 | all-reduce | flops 1024 | bytes 8192 | tf_op jit(solution)/shard_map/pmax | solution.py:24
  310.6 13.6 %psum.63 = f32[1024]{0:T(1024)S(1)} all-reduce(f32[1024]{0:T(1024)S(1)} %exponential_multiply_fusion), channel_id=1, replica_groups=mesh['parts'=2,'cols'=4,'rows'=2,'rep'=2] {'cols','rep'}, use_global_device_ids=true, to_apply=%region_91.92 | all-reduce | flops 1024 | bytes 8192 | tf_op jit(solution)/shard_map/psum | solution.py:25
  326.5 4.9 %pmax.134 = f32[256]{0:T(256)S(1)} all-reduce(f32[256]{0:T(256)S(1)} %get-tuple-element.855), channel_id=1, replica_groups=mesh['parts'=2,'cols'=4,'rows'=2,'rep'=2] {'rows'}, use_global_device_ids=true, to_apply=%region_96.97 | all-reduce | flops 256 | bytes 2048 | tf_op jit(solution)/shard_map/pmax | solution.py:30
  335.8 5.7 %while.222 = (s32[]{:T(128)}, f32[2,512]{1,0:T(2,128)S(1)}, f32[2,512]{1,0:T(2,128)S(1)}, f32[2,512,64]{1,0,2:T(2,128)S(1)}, f32[256]{0:T(256)S(1)}, /*index=5*/...) while((s32[]{:T(128)}, f32[2,512]{1,0:T(2,128)S(1)}, ...), condition=%wide.region_101.102_spmd, body=%wide.region_98.101_spmd.sunk | while | flops 202767360 | bytes 2647193 | solution.py:104
  342.1 13.6 %pmax.135 = f32[1024]{0:T(1024)S(1)} all-reduce(f32[1024]{0:T(1024)S(1)} %bitcast.434), channel_id=1, replica_groups=mesh['parts'=2,'cols'=4,'rows'=2,'rep'=2] {'cols','rep'}, use_global_device_ids=true, to_apply=%region_102.103 | all-reduce | flops 1024 | bytes 8192 | tf_op jit(solution)/shard_map/pmax | solution.py:108
  358.4 13.7 %all-reduce = f32[1024]{0:T(1024)S(1)} all-reduce(f32[1024]{0:T(1024)S(1)} %get-tuple-element.1408), channel_id=11, replica_groups=mesh['parts'=2,'cols'=4,'rows'=2,'rep'=2] {'cols','rep'}, use_global_device_ids=true, to_apply=%region_104.105.clone | all-reduce | flops 1024 | bytes 8192
  372.1 13.6 %reduce-scatter.2.cloned.1.call-done = f32[128,64]{0,1:T(8,128)} async-done(((f32[1024,64]{0,1:T(8,128)}), f32[128,64]{0,1:T(8,128)}) %reduce-scatter.2.cloned.1.call-update) | async-done | bytes 32784 | tf_op jit(solution)/shard_map/reduce_scatter | solution.py:111
  (360 shorter events, 87.0 us)
Async XLA Ops:
  7.2 1.2 copy-start.1
  7.2 378.5 %reduce-scatter.2.cloned.1.call-start = ((), (), s32[]{:S(2)}) async-start(), calls=%async_computation.1 | async-start | bytes 294912 | tf_op jit(solution)/shard_map/reduce_scatter | solution.py:111
  8.4 1.0 copy-start.2
  8.6 0.7 copy-start.4
  8.6 0.7 copy-start.6
  324.2 0.6 copy-start.3
  324.8 10.9 %copy-start = (f32[256,64]{0,1:T(8,128)S(1)}, f32[256,64]{0,1:T(8,128)}, u32[]{:S(2)}) copy-start(f32[256,64]{0,1:T(8,128)} %param.43) | copy-start | bytes 196612
  341.5 0.6 copy-start.5
  356.5 0.7 copy-start.7
Sparse Core Ops, SparseCore 0:
  356.6 29.0 reduce-scatter.1
